TPU v7x, 512 devices: a whole 4x4x16 slice. The times are simulated.
512 devices in a mesh: sec: 2 (over core), seq: 32 (over z, y_lo), rep: 8 (over x, y_hi).
Axes of the slice: x: 4, y: 4 (y_hi: 2, y_lo: 2; y = y_hi * 2 + y_lo), z: 16, core: 2. Of those that a mesh axis runs over, the one named last changes fastest.
Arguments:
- head_query: bfloat16 [64, 24, 1536, 128], P(('sec', 'rep'), None, 'seq'), may hold values from -4.5 to 4.5
- head_keys: bfloat16 [64, 24, 1536, 128], P(('sec', 'rep'), None, 'seq'), may hold values from -4.5 to 4.5
- head_values: bfloat16 [64, 24, 1536, 128], P(('sec', 'rep'), None, 'seq'), may hold values from -6 to 6
- mod_shift: float32 [64, 3072], P(('sec', 'rep')), may hold values from -3 to 3
- mod_scale: float32 [64, 3072], P(('sec', 'rep')), may hold values from -0.9 to 0.9
- final_weight: bfloat16 [3072, 64], replicated, may hold values from -0.109375 to 0.109375
- final_bias: float32 [64], replicated, may hold values from -3 to 3
- noisy_latent: float32 [64, 3, 64, 512], P(('sec', 'rep'), None, 'seq'), may hold values from -7.2 to 7.2
- step_index: int32 [64], P(('sec', 'rep')), may hold values from 46 to 49
- clip_order: int32 [64], replicated, may hold values from 0 to 63, each once
- conv_weight: bfloat16 [3, 3, 3, 16, 512], replicated, may hold values from -0.3125 to 0.3125
- conv_bias: float32 [512], replicated, may hold values from -3 to 3
- group_gain: float32 [512], replicated, may hold values from 0.1 to 1.9
- group_shift: float32 [512], replicated, may hold values from -3 to 3
Outputs:
- denoised: float32 [64, 3, 64, 512], P(('sec', 'rep'), None, 'seq')
- features: bfloat16 [64, 3, 64, 16384], P(('sec', 'rep'), None, 'seq')
All inputs are finite; a program needn't handle non-finite values.
Results may differ from a plain program's by a relative error of at most 0.005.
Values may be sent and summed in bfloat16 or wider, within the bound.
No kernel may reach another device: no remote copies, remote signals or barrier semaphores. Data moves between devices by JAX's collectives and lax.ppermute only.
A program may use at most 128 MiB of HBM per device.

v0:
```python
import math
import jax
import jax.numpy as jnp
from jax import lax
from jax.sharding import PartitionSpec as P

HEADS = 24
HEAD_DIM = 128
LAT_CH = 16
VAE_CH = 512
GROUPS = 32
FRAMES = 3
PATCH_W = 16
NSTEPS = 50
PATCH_OUT = 64
LAT_W = 32
eps_norm = 1e-06
shift_factor = 7.0


def extended(cells, sides, width):
    for axis, dim in sides:
        count = lax.axis_size(axis)
        ends = count - 1
        head = lax.slice_in_dim(cells, 0, width, axis=dim)
        tail = lax.slice_in_dim(cells, cells.shape[dim] - width, cells.shape[dim], axis=dim)
        cells = jnp.concatenate(
            [
                lax.ppermute(tail, axis, [(i, (i + 1) % count) for i in range(ends)]),
                cells,
                lax.ppermute(head, axis, [((i + 1) % count, i) for i in range(ends)]),
            ],
            axis=dim,
        )
    return cells


def attend_unit(operands):
    query_rows, key_rows, value_rows = operands
    length = query_rows.shape[0]
    block = math.gcd(length, 512)
    scale = 1.0 / math.sqrt(query_rows.shape[1])
    blocks = query_rows.reshape(length // block, block, query_rows.shape[1])

    def one_block(rows):
        scores = jnp.dot(rows, key_rows.T, preferred_element_type=jnp.float32) * scale
        top = jnp.max(scores, axis=1, keepdims=True)
        expd = jnp.exp(scores - top)
        weights = (expd / jnp.sum(expd, axis=1, keepdims=True)).astype(jnp.bfloat16)
        return jnp.dot(weights, value_rows, preferred_element_type=jnp.float32).astype(jnp.bfloat16)

    return lax.map(one_block, blocks).reshape(length, query_rows.shape[1])


def sigma_level(index):
    level = 1.0 - index.astype(jnp.float32) / NSTEPS
    return shift_factor * level / (1.0 + (shift_factor - 1.0) * level)


def causal_columns(rimmed):
    clips, frames, rows_rim, wide = rimmed.shape
    width = wide // LAT_CH
    grid = rimmed.reshape(clips, frames, rows_rim, width, LAT_CH)
    first = grid[:, :1]
    grid = jnp.concatenate([first, first, grid], axis=1)
    grid = jnp.pad(grid, ((0, 0), (0, 0), (0, 0), (1, 1), (0, 0)), mode="edge")
    taps = []
    for tap_time in range(3):
        for tap_row in range(3):
            for tap_col in range(3):
                taps.append(
                    grid[
                        :,
                        tap_time : tap_time + frames,
                        tap_row : tap_row + rows_rim - 2,
                        tap_col : tap_col + width,
                        :,
                    ]
                )
    return jnp.stack(taps, axis=4).reshape(clips, frames, rows_rim - 2, width, 27 * LAT_CH)


def edge_rows(rimmed):
    position = lax.axis_index("seq")
    last_index = lax.axis_size("seq") - 1
    upper = jnp.where(position == 0, rimmed[:, :, 1:2], rimmed[:, :, 0:1])
    lower = jnp.where(position == last_index, rimmed[:, :, -2:-1], rimmed[:, :, -1:])
    return jnp.concatenate([upper, rimmed[:, :, 1:-1], lower], axis=2)


def shards(
    head_query,
    head_keys,
    head_values,
    mod_shift,
    mod_scale,
    final_weight,
    final_bias,
    noisy_latent,
    step_index,
    clip_order,
    conv_weight,
    conv_bias,
    group_gain,
    group_shift,
):
    n_seq = lax.axis_size("seq")
    clips = head_query.shape[0]
    tok_dev = head_query.shape[2]
    units_local = clips * HEADS // n_seq
    query_four = head_query.reshape(n_seq, units_local, tok_dev, HEAD_DIM)
    keys_four = head_keys.reshape(n_seq, units_local, tok_dev, HEAD_DIM)
    values_four = head_values.reshape(n_seq, units_local, tok_dev, HEAD_DIM)
    query_part = lax.all_to_all(query_four, "seq", split_axis=0, concat_axis=2, tiled=True)
    keys_part = lax.all_to_all(keys_four, "seq", split_axis=0, concat_axis=2, tiled=True)
    values_part = lax.all_to_all(values_four, "seq", split_axis=0, concat_axis=2, tiled=True)
    outputs = lax.map(attend_unit, (query_part[0], keys_part[0], values_part[0]))[None]
    mixed = lax.all_to_all(outputs, "seq", split_axis=2, concat_axis=0, tiled=True)
    weights3 = final_weight.astype(jnp.float32).reshape(HEADS, HEAD_DIM, PATCH_OUT)
    scale3 = mod_scale.reshape(clips, HEADS, HEAD_DIM)
    shift3 = mod_shift.reshape(clips, HEADS, HEAD_DIM)
    heads = mixed.reshape(clips, HEADS, tok_dev, HEAD_DIM).astype(jnp.float32)
    mean = jnp.mean(heads, axis=(1, 3), keepdims=True)
    spread = jnp.mean(jnp.square(heads - mean), axis=(1, 3), keepdims=True)
    normed = (heads - mean) * lax.rsqrt(spread + eps_norm)
    modulated = normed * (1.0 + scale3[:, :, None, :]) + shift3[:, :, None, :]
    velocity = (
        jnp.einsum("chtd,hdo->cto", modulated, weights3, precision=lax.Precision.HIGHEST)
        + final_bias
    )
    rows_dev = noisy_latent.shape[2]
    velocity = velocity.reshape(clips, rows_dev // 2, FRAMES, PATCH_W, 2, 2, LAT_CH)
    velocity = jnp.transpose(velocity, (0, 2, 1, 4, 3, 5, 6)).reshape(noisy_latent.shape)
    step = sigma_level(step_index + 1) - sigma_level(step_index)
    denoised = noisy_latent + step[:, None, None, None] * velocity
    decoder_in = denoised.astype(jnp.bfloat16)
    group_index = lax.axis_index(("sec", "rep"))
    wanted = lax.dynamic_slice_in_dim(clip_order, group_index * clips, clips)
    everyone = lax.all_gather(decoder_in, ("sec", "rep"), axis=0, tiled=True)
    picked = jnp.take(everyone, wanted, axis=0)
    rimmed = edge_rows(extended(picked, (("seq", 2),), 1))
    columns = causal_columns(rimmed)
    flat_weight = conv_weight.reshape(27 * LAT_CH, VAE_CH)
    conv_out = (
        jnp.dot(columns.reshape(-1, 27 * LAT_CH), flat_weight, preferred_element_type=jnp.float32)
        + conv_bias
    )
    conv_out = conv_out.reshape(clips, -1, GROUPS, VAE_CH // GROUPS)
    cells = conv_out.shape[1] * n_seq * (VAE_CH // GROUPS)
    local_sum = jnp.sum(conv_out, axis=(1, 3))
    mean = lax.psum(local_sum, "seq") / cells
    centered = conv_out - mean[:, None, :, None]
    spread = lax.psum(jnp.sum(jnp.square(centered), axis=(1, 3)), "seq") / cells
    normed = (centered * lax.rsqrt(spread + eps_norm)[:, None, :, None]).reshape(clips, -1, VAE_CH)
    features = jax.nn.silu(normed * group_gain + group_shift).astype(jnp.bfloat16)
    features = features.reshape(clips, FRAMES, rows_dev, LAT_W * VAE_CH)
    return (denoised, features)


def solution(mesh):
    placed = (
        P(("sec", "rep"), None, "seq", None),
        P(("sec", "rep"), None, "seq", None),
        P(("sec", "rep"), None, "seq", None),
        P(("sec", "rep"), None),
        P(("sec", "rep"), None),
        P(),
        P(),
        P(("sec", "rep"), None, "seq", None),
        P(("sec", "rep")),
        P(),
        P(),
        P(),
        P(),
        P(),
    )
    return jax.shard_map(
        shards,
        mesh=mesh,
        in_specs=placed,
        out_specs=(P(("sec", "rep"), None, "seq", None), P(("sec", "rep"), None, "seq", None)),
        check_vma=False,
    )
```

profile of v0, /device:TPU:8, one launch (start us, length us, event | category | flops | bytes accessed | tf_op | source)
XLA Modules:
  0.0 569.3 jit_solution(6883211467850710125)
XLA Ops:
  0.7 77.9 %all_to_all.54 = bf16[32,3,48,128]{3,2,1,0:T(8,128)(2,1)} all-to-all(bf16[32,3,48,128]{3,2,1,0:T(8,128)(2,1)} %bitcast.227), channel_id=1, replica_groups=mesh['sec'=2,'seq'=32,'rep'=8] {'seq'}, dimensions={0} | all-to-all | bytes 2359296 | tf_op jit(solution)/shard_map/all_to_all | solution.py:114
  78.5 64.2 %all_to_all.55 = bf16[32,3,48,128]{3,2,1,0:T(8,128)(2,1)} all-to-all(bf16[32,3,48,128]{3,2,1,0:T(8,128)(2,1)S(1)} %bitcast.228), channel_id=1, replica_groups=mesh['sec'=2,'seq'=32,'rep'=8] {'seq'}, dimensions={0} | all-to-all | bytes 2359296 | tf_op jit(solution)/shard_map/all_to_all | solution.py:115
  142.7 4.2 all-to-all-start.2
  146.9 1.4 copy.116
  148.5 1.1 copy.117
  149.6 55.0 %all-to-all-done.2 = bf16[32,3,48,128]{3,2,1,0:T(8,128)(2,1)S(1)} async-done(((bf16[32,3,48,128]{3,2,1,0:T(8,128)(2,1)}), bf16[32,3,48,128]{3,2,1,0:T(8,128)(2,1)S(1)}, u32[]{:S(2)}, u32[]{:S(2)}) %all-to-all-start.2) | async-done | bytes 1179680 | tf_op jit(solution)/shard_map/all_to_all | solution.py:116
  204.6 1.1 copy.118
  205.8 24.2 %while.21 = (s32[]{:T(128)}, bf16[3,1536,128]{2,1,0:T(8,128)(2,1)}, bf16[3,1536,128]{2,1,0:T(8,128)(2,1)S(1)}, bf16[3,1536,128]{2,1,0:T(8,128)(2,1)}, bf16[3,153...) while((s32[]{:T(128)}, bf16[3,1536,128]{2,1,0:T(8,128)(2,1)}, ...), condition=%wide.region_5.6_spmd, body=%wide.region_0.5_spmd.sunk | while | flops 408222720 | bytes 13641974 | solution.py:117
  205.8 1.2 dynamic-slice_bitcast_fusion.3
  207.0 6.1 %while.22 = (s32[]{:T(128)}, bf16[3,512,128]{2,1,0:T(8,128)(2,1)S(1)}, bf16[3,512,128]{2,1,0:T(8,128)(2,1)S(1)}, bf16[1536,128]{1,0:T(8,128)(2,1)S(1)}, bf16[1536,128]{1,0:T(8,128)(2,1)S(1)}, /*index=5*/s32[]{:T(128)}) while((s32[]{:T(128)}, bf16[3,512,128]{2,1,0:T(8,128)(2,1)S(1)}, bf16[3,512,128]{2,1,0:T(8,128)(2,1)S(1)}, ...), condition=%wide.region_4.4_spmd, body=%wide.region_1.3_spmd.sunk | while | flops 408222720 | bytes 10496085 | solution.py:52
  208.2 0.8 fusion.89
  210.2 0.8 fusion.89
  212.2 0.8 fusion.89
  213.0 0.8 bitcast_dynamic-update-slice_fusion.2
  213.8 1.2 dynamic-slice_bitcast_fusion.3
  215.0 6.1 %while.22 = (s32[]{:T(128)}, bf16[3,512,128]{2,1,0:T(8,128)(2,1)S(1)}, bf16[3,512,128]{2,1,0:T(8,128)(2,1)S(1)}, bf16[1536,128]{1,0:T(8,128)(2,1)S(1)}, bf16[1536,128]{1,0:T(8,128)(2,1)S(1)}, /*index=5*/s32[]{:T(128)}) while((s32[]{:T(128)}, bf16[3,512,128]{2,1,0:T(8,128)(2,1)S(1)}, bf16[3,512,128]{2,1,0:T(8,128)(2,1)S(1)}, ...), condition=%wide.region_4.4_spmd, body=%wide.region_1.3_spmd.sunk | while | flops 408222720 | bytes 10496085 | solution.py:52
  216.3 0.8 fusion.89
  218.3 0.8 fusion.89
  220.3 0.8 fusion.89
  221.1 0.8 bitcast_dynamic-update-slice_fusion.2
  221.9 1.2 dynamic-slice_bitcast_fusion.3
  223.1 6.1 %while.22 = (s32[]{:T(128)}, bf16[3,512,128]{2,1,0:T(8,128)(2,1)S(1)}, bf16[3,512,128]{2,1,0:T(8,128)(2,1)S(1)}, bf16[1536,128]{1,0:T(8,128)(2,1)S(1)}, bf16[1536,128]{1,0:T(8,128)(2,1)S(1)}, /*index=5*/s32[]{:T(128)}) while((s32[]{:T(128)}, bf16[3,512,128]{2,1,0:T(8,128)(2,1)S(1)}, bf16[3,512,128]{2,1,0:T(8,128)(2,1)S(1)}, ...), condition=%wide.region_4.4_spmd, body=%wide.region_1.3_spmd.sunk | while | flops 408222720 | bytes 10496085 | solution.py:52
  224.3 0.8 fusion.89
  226.3 0.8 fusion.89
  228.4 0.8 fusion.89
  229.1 0.8 bitcast_dynamic-update-slice_fusion.2
  229.9 8.1 %copy.141 = bf16[3,1536,128]{2,0,1:T(4,128)(2,1)} copy(bf16[3,1536,128]{2,1,0:T(8,128)(2,1)} %get-tuple-element.56) | data formatting | bytes 2359296 | tf_op jit(solution)/shard_map/while | solution.py:117
  238.1 5.7 all-to-all-start.3
  243.9 76.1 %all-to-all-done.3 = bf16[1,3,1536,128]{3,1,0,2:T(4,128)(2,1)S(1)} async-done(((bf16[1,3,1536,128]{3,1,0,2:T(4,128)(2,1)}), bf16[1,3,1536,128]{3,1,0,2:T(4,128)(2,1)S(1)}, u32[]{:S(2)}, u32[]{:S(2)}) %all-to-all-start.3) | async-done | bytes 1179680 | tf_op jit(solution)/shard_map/all_to_all | solution.py:118
  320.4 3.1 fusion.19
  323.7 22.0 %multiply_reduce_fusion = f32[32,48]{1,0:T(8,128)S(1)} fusion(bf16[1,3,32,48,128]{4,1,3,2,0:T(4,128)(2,1)S(1)} %bitcast.219, f32[32,48]{1,0:T(8,128)S(1)} %broadcast_bitcast_fusion.2), kind=kLoop, calls=%fused_computation.17 | loop fusion | flops 2357760 | bytes 1191936 | tf_op jit(solution)/shard_map/reduce_sum | solution.py:124
  345.8 1.6 fusion.28
  348.4 0.7 fusion.72
  349.2 36.8 %all_gather.3 = bf16[64,3,2,512]{3,2,1,0:T(2,128)(2,1)S(1)} all-gather(bf16[4,3,2,512]{3,2,1,0:T(2,128)(2,1)S(1)} %get-tuple-element.79), channel_id=1, replica_groups=mesh['sec'=2,'seq'=32,'rep'=8] {'sec','rep'}, dimensions={0}, use_global_device_ids=true | all-gather | bytes 417792 | tf_op jit(solution)/shard_map/all_gather | solution.py:139
  386.7 3.1 collective-permute-start
  389.8 3.0 collective-permute-start.1
  392.8 3.5 collective-permute-done.1
  398.7 0.7 fusion.69
  400.1 0.7 fusion.67
  400.9 0.7 fusion.66
  402.3 0.7 fusion.40
  403.0 0.7 fusion.64
  404.4 0.7 fusion.48
  405.1 0.7 fusion.62
  406.6 0.7 fusion.45
  407.3 0.7 fusion.60
  408.0 0.7 fusion.59
  408.7 0.7 fusion.42
  409.4 0.7 fusion.58
  411.6 0.7 fusion.55
  413.7 0.7 fusion.52
  415.8 0.7 fusion.49
  416.5 7.9 %copy.123 = bf16[4,3,2,32,27,16]{3,2,1,0,5,4:T(2,128)(2,1)S(1)} copy(bf16[4,3,2,32,27,16]{5,3,2,1,0,4:T(8,128)(2,1)} %fusion.49) | data formatting | bytes 1327104 | tf_op jit(solution)/shard_map/stack | solution.py:80
  424.5 2.5 reshape_reshape.3
  427.0 1.7 convolution_add_fusion
  428.7 1.6 copy.124
  430.3 2.5 reshape.109
  432.8 2.7 reshape.110
  436.0 59.9 %psum.14 = f32[4,32]{1,0:T(4,128)S(1)} all-reduce(f32[4,32]{1,0:T(4,128)S(1)} %copy.125), channel_id=1, replica_groups=mesh['sec'=2,'seq'=32,'rep'=8] {'seq'}, use_global_device_ids=true, to_apply=%region_11.12 | all-reduce | flops 128 | bytes 1024 | tf_op jit(solution)/shard_map/psum | solution.py:151
  496.0 0.8 multiply_reduce_fusion.1
  496.8 62.3 %psum.15 = f32[4,32]{1,0:T(4,128)S(1)} all-reduce(f32[4,32]{1,0:T(4,128)S(1)} %copy.127), channel_id=1, replica_groups=mesh['sec'=2,'seq'=32,'rep'=8] {'seq'}, use_global_device_ids=true, to_apply=%region_13.14 | all-reduce | flops 128 | bytes 1024 | tf_op jit(solution)/shard_map/psum | solution.py:153
  559.5 2.5 mul.94
  562.3 2.5 sub.70
  564.8 4.5 fusion.20
  (104 shorter events, 24.5 us)
Async XLA Ops:
  0.6 426.3 %copy-start = (bf16[3,3,3,16,512]{4,3,2,1,0:T(8,128)(2,1)S(1)}, bf16[3,3,3,16,512]{4,3,2,1,0:T(8,128)(2,1)}, u32[]{:S(2)}) copy-start(bf16[3,3,3,16,512]{4,3,2,1,0:T(8,128)(2,1)} %param.28) | copy-start | bytes 1327108
  0.6 77.9 %copy-start.2 = (bf16[4,24,48,128]{3,2,1,0:T(8,128)(2,1)S(1)}, bf16[4,24,48,128]{3,2,1,0:T(8,128)(2,1)}, u32[]{:S(2)}) copy-start(bf16[4,24,48,128]{3,2,1,0:T(8,128)(2,1)} %param.19) | copy-start | bytes 3538948
  142.7 61.9 %all-to-all-start.2 = ((bf16[32,3,48,128]{3,2,1,0:T(8,128)(2,1)}), bf16[32,3,48,128]{3,2,1,0:T(8,128)(2,1)S(1)}, u32[]{:S(2)}, u32[]{:S(2)}) async-start(bf16[32,3,48,128]{3,2,1,0:T(8,128)(2,1)} %bitcast.14), calls=%async_computation.2 | async-start | bytes 2359296 | tf_op jit(solution)/shard_map/all_to_all | solution.py:116
  146.9 1.6 copy-start.1
  229.9 13.8 %copy-start.8 = (s32[64]{0:T(128)S(1)}, s32[64]{0:T(128)}, u32[]{:S(2)}) copy-start(s32[64]{0:T(128)} %param.27) | copy-start | bytes 772
  229.9 13.9 %copy-start.11 = (s32[4]{0:T(128)S(1)}, s32[4]{0:T(128)}, u32[]{:S(2)}) copy-start(s32[4]{0:T(128)} %param.26) | copy-start | bytes 52
  229.9 13.9 %copy-start.6 = (f32[512]{0:T(512)S(1)}, f32[512]{0:T(512)}, u32[]{:S(2)}) copy-start(f32[512]{0:T(512)} %param.31) | copy-start | bytes 6148
  229.9 14.0 %copy-start.3 = (f32[4,3072]{1,0:T(4,128)S(1)}, f32[4,3072]{1,0:T(4,128)}, u32[]{:S(2)}) copy-start(f32[4,3072]{1,0:T(4,128)} %param.22) | copy-start | bytes 147460
  229.9 14.0 %copy-start.4 = (f32[4,3072]{1,0:T(4,128)S(1)}, f32[4,3072]{1,0:T(4,128)}, u32[]{:S(2)}) copy-start(f32[4,3072]{1,0:T(4,128)} %param.21) | copy-start | bytes 147460
  238.1 82.0 %all-to-all-start.3 = ((bf16[1,3,1536,128]{3,1,0,2:T(4,128)(2,1)}), bf16[1,3,1536,128]{3,1,0,2:T(4,128)(2,1)S(1)}, u32[]{:S(2)}, u32[]{:S(2)}) async-start(bf16[1,3,1536,128]{3,1,0,2:T(4,128)(2,1)} %bitcast.224), calls=%async_computation.3 | async-start | bytes 3145728 | tf_op jit(solution)/shard_map/all_to_all | solution.py:118
  323.5 22.3 %copy-start.9 = (bf16[3072,64]{0,1:T(8,128)(2,1)S(1)}, bf16[3072,64]{0,1:T(8,128)(2,1)}, u32[]{:S(2)}) copy-start(bf16[3072,64]{0,1:T(8,128)(2,1)} %param.23) | copy-start | bytes 1179652
  323.5 22.3 %copy-start.12 = (f32[64]{0:T(128)S(1)}, f32[64]{0:T(128)}, u32[]{:S(2)}) copy-start(f32[64]{0:T(128)} %param.24) | copy-start | bytes 772
  323.7 24.7 %copy-start.5 = (f32[4,3,2,512]{3,2,1,0:T(2,128)S(1)}, f32[4,3,2,512]{3,2,1,0:T(2,128)}, u32[]{:S(2)}) copy-start(f32[4,3,2,512]{3,2,1,0:T(2,128)} %param.25) | copy-start | bytes 147460
  345.8 47.0 %copy-start.7 = (f32[512]{0:T(512)S(1)}, f32[512]{0:T(512)}, u32[]{:S(2)}) copy-start(f32[512]{0:T(512)} %param.30) | copy-start | bytes 6148
  386.7 6.2 %collective-permute-start = (bf16[4,3,1,512]{3,2,1,0:T(2,128)(2,1)S(1)}, bf16[4,3,1,512]{3,2,1,0:T(2,128)(2,1)S(1)}, u32[]{:S(2)}, u32[]{:S(2)}) collective-permute-start(bf16[4,3,1,512]{3,2,1,0:T(2,128)(2,1)S(1)} %get-tuple-element.89), channel_id=1, source_target_pairs={{0,8},{8,16},{16,24},{24,32},{32,40},{40,48},{48,56},{56,64},{64,7... | collective-permute-start | bytes 36872 | tf_op jit(solution)/shard_map/ppermute | solution.py:29
  389.8 6.6 %collective-permute-start.1 = (bf16[4,3,1,512]{3,2,1,0:T(2,128)(2,1)S(1)}, bf16[4,3,1,512]{3,2,1,0:T(2,128)(2,1)S(1)}, u32[]{:S(2)}, u32[]{:S(2)}) collective-permute-start(bf16[4,3,1,512]{3,2,1,0:T(2,128)(2,1)S(1)} %get-tuple-element.90), channel_id=1, source_target_pairs={{8,0},{16,8},{24,16},{32,24},{40,32},{48,40},{56,48},{64,56},{72,6... | collective-permute-start | bytes 36872 | tf_op jit(solution)/shard_map/ppermute | solution.py:31
  424.4 2.5 copy-start.10
where the time goes:
time: 570 us; the launch traced here: 569 us
  blocking collectives  301 us (53%)
  waiting for transfers between devices  135 us (24%)
  local copies, waits for them, and re-layouts  58.9 us (10%)
  other arithmetic  41.5 us (7%)
  matrix products  16.1 us (3%)
  starting transfers between devices  15.9 us (3%)
    all_to_all x1, blocking collectives, shards(): lax.all_to_all(query_four, 'seq', split_axis=0, concat_axis=2, tiled=True)  77.9 us
    all_to_all x1, waiting for transfers between devices, shards(): lax.all_to_all(outputs, 'seq', split_axis=2, concat_axis=0, tiled=True)  76.1 us
    all_to_all x1, blocking collectives, shards(): lax.all_to_all(keys_four, 'seq', split_axis=0, concat_axis=2, tiled=True)  64.2 us
    psum x1, blocking collectives, shards(): spread = lax.psum(jnp.sum(jnp.square(centered), axis=(1, 3)), 'seq') / cells  62.3 us
    psum x1, blocking collectives, shards(): mean = lax.psum(local_sum, 'seq') / cells  59.9 us
    all_to_all x1, waiting for transfers between devices, shards(): lax.all_to_all(values_four, 'seq', split_axis=0, concat_axis=2, tiled=True)  55 us
    all_gather x1, blocking collectives, shards(): everyone = lax.all_gather(decoder_in, ('sec', 'rep'), axis=0, tiled=True)  36.8 us
    reduce_sum x2, other arithmetic, shards(): spread = jnp.mean(jnp.square(heads - mean), axis=(1, 3), keepdims=True)  22 us
  transfers between devices with their start and end apart: 4, of which 3 were waited for; matrix products, arithmetic and copies ran while one was open for 0% of the time, Pallas kernels for 0%

commit v1 on v0

--- a/solution.py
+++ b/solution.py
@@ -16,6 +16,14 @@
 LAT_W = 32
 eps_norm = 1e-06
 shift_factor = 7.0
+
+
+def connect_the_squares(m):
+    e_now = jnp.split(m, lax.axis_size("seq"), axis=0)
+    h_now = jnp.stack(e_now, axis=0)
+    prior = lax.all_to_all(h_now, "seq", split_axis=0, concat_axis=0)
+    k_now = jnp.concatenate(prior, axis=2)
+    return k_now
 
 
 def extended(cells, sides, width):
@@ -112,7 +120,7 @@
     keys_four = head_keys.reshape(n_seq, units_local, tok_dev, HEAD_DIM)
     values_four = head_values.reshape(n_seq, units_local, tok_dev, HEAD_DIM)
     query_part = lax.all_to_all(query_four, "seq", split_axis=0, concat_axis=2, tiled=True)
-    keys_part = lax.all_to_all(keys_four, "seq", split_axis=0, concat_axis=2, tiled=True)
+    keys_part = connect_the_squares(keys_four)
     values_part = lax.all_to_all(values_four, "seq", split_axis=0, concat_axis=2, tiled=True)
     outputs = lax.map(attend_unit, (query_part[0], keys_part[0], values_part[0]))[None]
     mixed = lax.all_to_all(outputs, "seq", split_axis=2, concat_axis=0, tiled=True)

time: 570 us -> 574 us (level)
  the two profiles are of different devices: /device:TPU:8 before, /device:TPU:6 now
where the time goes in v1:
time: 574 us; the launch traced here: 571 us
  blocking collectives  225 us (39%)
  waiting for transfers between devices  169 us (29%)
  local copies, waits for them, and re-layouts  84.7 us (15%)
  other arithmetic  41.5 us (7%)
  starting transfers between devices  33.4 us (6%)
  matrix products  16.1 us (3%)
    all_to_all x1, waiting for transfers between devices, shards(): lax.all_to_all(outputs, 'seq', split_axis=2, concat_axis=0, tiled=True)  74.3 us
    all_to_all x1, blocking collectives, connect_the_squares(): prior = lax.all_to_all(h_now, 'seq', split_axis=0, concat_axis=0)  66.3 us
    psum x1, blocking collectives, shards(): mean = lax.psum(local_sum, 'seq') / cells  61.4 us
    psum x1, blocking collectives, shards(): spread = lax.psum(jnp.sum(jnp.square(centered), axis=(1, 3)), 'seq') / cells  60.8 us
    all_to_all x1, waiting for transfers between devices, shards(): lax.all_to_all(values_four, 'seq', split_axis=0, concat_axis=2, tiled=True)  55.9 us
    unnamed x78, local copies, waits for them, and re-layouts  39 us
    all_gather x1, blocking collectives, shards(): everyone = lax.all_gather(decoder_in, ('sec', 'rep'), axis=0, tiled=True)  37 us
    all_to_all x1, waiting for transfers between devices, shards(): lax.all_to_all(query_four, 'seq', split_axis=0, concat_axis=2, tiled=True)  34.2 us
  transfers between devices with their start and end apart: 5, of which 4 were waited for; matrix products, arithmetic and copies ran while one was open for 5% of the time, Pallas kernels for 0%

profile of v1, /device:TPU:6, one launch (start us, length us, event | category | flops | bytes accessed | tf_op | source)
XLA Modules:
  0.0 571.0 jit_solution(17472371444419194063)
XLA Ops:
  0.6 16.6 %all-to-all-start = ((bf16[32,3,48,128]{3,2,1,0:T(8,128)(2,1)}), bf16[32,3,48,128]{3,2,1,0:T(8,128)(2,1)S(1)}, u32[]{:S(2)}, u32[]{:S(2)}) async-start(bf16[32,3,48,128]{3,2,1,0:T(8,128)(2,1)} %bitcast.385), calls=%async_computation | async-start | bytes 2359296 | tf_op jit(solution)/shard_map/all_to_all | solution.py:122
  18.1 0.8 constant_dynamic-update-slice_fusion.30
  18.8 0.8 constant_dynamic-update-slice_fusion.29
  19.6 0.8 constant_dynamic-update-slice_fusion.28
  20.4 0.8 constant_dynamic-update-slice_fusion.27
  21.2 0.8 constant_dynamic-update-slice_fusion.26
  21.9 0.8 constant_dynamic-update-slice_fusion.25
  22.7 0.8 constant_dynamic-update-slice_fusion.24
  23.5 0.8 constant_dynamic-update-slice_fusion.23
  24.3 0.8 constant_dynamic-update-slice_fusion.22
  25.1 0.8 constant_dynamic-update-slice_fusion.21
  25.8 0.8 constant_dynamic-update-slice_fusion.20
  26.6 0.8 constant_dynamic-update-slice_fusion.19
  27.4 0.8 constant_dynamic-update-slice_fusion.18
  28.2 0.8 constant_dynamic-update-slice_fusion.17
  28.9 0.8 constant_dynamic-update-slice_fusion.16
  29.7 0.8 constant_dynamic-update-slice_fusion.15
  30.5 0.8 constant_dynamic-update-slice_fusion.14
  32.0 0.8 constant_dynamic-update-slice_fusion.12
  32.8 0.8 constant_dynamic-update-slice_fusion.11
  33.6 0.8 constant_dynamic-update-slice_fusion.10
  34.4 0.8 constant_dynamic-update-slice_fusion.9
  35.2 0.8 constant_dynamic-update-slice_fusion.8
  35.9 0.8 constant_dynamic-update-slice_fusion.7
  36.7 0.8 constant_dynamic-update-slice_fusion.6
  39.0 0.8 constant_dynamic-update-slice_fusion.3
  39.8 0.8 constant_dynamic-update-slice_fusion.2
  40.6 0.8 constant_dynamic-update-slice_fusion.1
  41.4 0.8 constant_dynamic-update-slice_fusion
  42.1 34.2 %all-to-all-done = bf16[32,3,48,128]{3,2,1,0:T(8,128)(2,1)S(1)} async-done(((bf16[32,3,48,128]{3,2,1,0:T(8,128)(2,1)}), bf16[32,3,48,128]{3,2,1,0:T(8,128)(2,1)S(1)}, u32[]{:S(2)}, u32[]{:S(2)}) %all-to-all-start) | async-done | bytes 1179680 | tf_op jit(solution)/shard_map/all_to_all | solution.py:122
  76.4 66.3 %all_to_all.44 = bf16[32,1,3,48,128]{4,3,2,1,0:T(8,128)(2,1)} all-to-all(bf16[32,1,3,48,128]{4,3,2,1,0:T(8,128)(2,1)S(1)} %constant_dynamic-update-slice_fusion), channel_id=1, replica_groups=mesh['sec'=2,'seq'=32,'rep'=8] {'seq'}, dimensions={0} | all-to-all | bytes 2359296 | tf_op jit(solution)/shard_map/all_to_all | solution.py:24
  142.7 4.7 all-to-all-start.2
  147.4 2.4 copy.177
  149.8 55.9 %all-to-all-done.2 = bf16[32,3,48,128]{3,2,1,0:T(8,128)(2,1)} async-done(((bf16[32,3,48,128]{3,2,1,0:T(8,128)(2,1)}), bf16[32,3,48,128]{3,2,1,0:T(8,128)(2,1)}, u32[]{:S(2)}, u32[]{:S(2)}) %all-to-all-start.2) | async-done | bytes 1179680 | tf_op jit(solution)/shard_map/all_to_all | solution.py:124
  205.6 2.4 copy.178
  208.0 24.2 %while.21 = (s32[]{:T(128)}, bf16[3,1536,128]{2,1,0:T(8,128)(2,1)}, bf16[3,1536,128]{2,1,0:T(8,128)(2,1)S(1)}, bf16[3,1536,128]{2,1,0:T(8,128)(2,1)}, bf16[3,153...) while((s32[]{:T(128)}, bf16[3,1536,128]{2,1,0:T(8,128)(2,1)}, ...), condition=%wide.region_5.6_spmd, body=%wide.region_0.5_spmd.sunk | while | flops 408222720 | bytes 13641974 | solution.py:125
  208.1 1.2 dynamic-slice_bitcast_fusion.3
  209.3 6.1 %while.22 = (s32[]{:T(128)}, bf16[3,512,128]{2,1,0:T(8,128)(2,1)S(1)}, bf16[3,512,128]{2,1,0:T(8,128)(2,1)S(1)}, bf16[1536,128]{1,0:T(8,128)(2,1)S(1)}, bf16[1536,128]{1,0:T(8,128)(2,1)S(1)}, /*index=5*/s32[]{:T(128)}) while((s32[]{:T(128)}, bf16[3,512,128]{2,1,0:T(8,128)(2,1)S(1)}, bf16[3,512,128]{2,1,0:T(8,128)(2,1)S(1)}, ...), condition=%wide.region_4.4_spmd, body=%wide.region_1.3_spmd.sunk | while | flops 408222720 | bytes 10496085 | solution.py:60
  216.1 1.2 dynamic-slice_bitcast_fusion.3
  217.3 6.1 %while.22 = (s32[]{:T(128)}, bf16[3,512,128]{2,1,0:T(8,128)(2,1)S(1)}, bf16[3,512,128]{2,1,0:T(8,128)(2,1)S(1)}, bf16[1536,128]{1,0:T(8,128)(2,1)S(1)}, bf16[1536,128]{1,0:T(8,128)(2,1)S(1)}, /*index=5*/s32[]{:T(128)}) while((s32[]{:T(128)}, bf16[3,512,128]{2,1,0:T(8,128)(2,1)S(1)}, bf16[3,512,128]{2,1,0:T(8,128)(2,1)S(1)}, ...), condition=%wide.region_4.4_spmd, body=%wide.region_1.3_spmd.sunk | while | flops 408222720 | bytes 10496085 | solution.py:60
  223.4 0.8 bitcast_dynamic-update-slice_fusion.2
  224.2 1.2 dynamic-slice_bitcast_fusion.3
  225.4 6.1 %while.22 = (s32[]{:T(128)}, bf16[3,512,128]{2,1,0:T(8,128)(2,1)S(1)}, bf16[3,512,128]{2,1,0:T(8,128)(2,1)S(1)}, bf16[1536,128]{1,0:T(8,128)(2,1)S(1)}, bf16[1536,128]{1,0:T(8,128)(2,1)S(1)}, /*index=5*/s32[]{:T(128)}) while((s32[]{:T(128)}, bf16[3,512,128]{2,1,0:T(8,128)(2,1)S(1)}, bf16[3,512,128]{2,1,0:T(8,128)(2,1)S(1)}, ...), condition=%wide.region_4.4_spmd, body=%wide.region_1.3_spmd.sunk | while | flops 408222720 | bytes 10496085 | solution.py:60
  232.2 8.1 %copy.201 = bf16[3,1536,128]{2,0,1:T(4,128)(2,1)} copy(bf16[3,1536,128]{2,1,0:T(8,128)(2,1)} %get-tuple-element.56) | data formatting | bytes 2359296 | tf_op jit(solution)/shard_map/while | solution.py:125
  240.3 5.4 all-to-all-start.3
  245.9 74.3 %all-to-all-done.3 = bf16[1,3,1536,128]{3,1,0,2:T(4,128)(2,1)S(1)} async-done(((bf16[1,3,1536,128]{3,1,0,2:T(4,128)(2,1)}), bf16[1,3,1536,128]{3,1,0,2:T(4,128)(2,1)S(1)}, u32[]{:S(2)}, u32[]{:S(2)}) %all-to-all-start.3) | async-done | bytes 1179680 | tf_op jit(solution)/shard_map/all_to_all | solution.py:126
  320.6 3.1 fusion.19
  323.9 22.0 %multiply_reduce_fusion = f32[32,48]{1,0:T(8,128)S(1)} fusion(bf16[1,3,32,48,128]{4,1,3,2,0:T(4,128)(2,1)S(1)} %bitcast.345, f32[32,48]{1,0:T(8,128)S(1)} %broadcast_bitcast_fusion.2), kind=kLoop, calls=%fused_computation.17 | loop fusion | flops 2357760 | bytes 1191936 | tf_op jit(solution)/shard_map/reduce_sum | solution.py:132
  346.0 1.6 fusion.28
  349.4 37.0 %all_gather.3 = bf16[64,3,2,512]{3,2,1,0:T(2,128)(2,1)S(1)} all-gather(bf16[4,3,2,512]{3,2,1,0:T(2,128)(2,1)S(1)} %get-tuple-element.79), channel_id=1, replica_groups=mesh['sec'=2,'seq'=32,'rep'=8] {'sec','rep'}, dimensions={0}, use_global_device_ids=true | all-gather | bytes 417792 | tf_op jit(solution)/shard_map/all_gather | solution.py:147
  387.2 5.2 collective-permute-start
  392.3 1.5 collective-permute-start.1
  394.0 4.1 collective-permute-done.1
  418.2 7.9 %copy.183 = bf16[4,3,2,32,27,16]{3,2,1,0,5,4:T(2,128)(2,1)S(1)} copy(bf16[4,3,2,32,27,16]{5,3,2,1,0,4:T(8,128)(2,1)} %fusion.49) | data formatting | bytes 1327104 | tf_op jit(solution)/shard_map/stack | solution.py:88
  426.1 2.5 reshape_reshape.3
  428.6 1.7 convolution_add_fusion
  430.3 1.6 copy.184
  431.9 2.5 reshape.112
  434.4 2.7 reshape.113
  437.7 61.4 %psum.14 = f32[4,32]{1,0:T(4,128)S(1)} all-reduce(f32[4,32]{1,0:T(4,128)S(1)} %copy.185), channel_id=1, replica_groups=mesh['sec'=2,'seq'=32,'rep'=8] {'seq'}, use_global_device_ids=true, to_apply=%region_11.12 | all-reduce | flops 128 | bytes 1024 | tf_op jit(solution)/shard_map/psum | solution.py:159
  500.0 60.8 %psum.15 = f32[4,32]{1,0:T(4,128)S(1)} all-reduce(f32[4,32]{1,0:T(4,128)S(1)} %copy.187), channel_id=1, replica_groups=mesh['sec'=2,'seq'=32,'rep'=8] {'seq'}, use_global_device_ids=true, to_apply=%region_13.14 | all-reduce | flops 128 | bytes 1024 | tf_op jit(solution)/shard_map/psum | solution.py:161
  561.2 2.5 mul.94
  564.0 2.5 sub.70
  566.5 4.5 fusion.20
  (133 shorter events, 48.4 us)
Async XLA Ops:
  0.6 428.0 %copy-start = (bf16[3,3,3,16,512]{4,3,2,1,0:T(8,128)(2,1)S(1)}, bf16[3,3,3,16,512]{4,3,2,1,0:T(8,128)(2,1)}, u32[]{:S(2)}) copy-start(bf16[3,3,3,16,512]{4,3,2,1,0:T(8,128)(2,1)} %param.28) | copy-start | bytes 1327108
  0.6 75.7 %all-to-all-start = ((bf16[32,3,48,128]{3,2,1,0:T(8,128)(2,1)}), bf16[32,3,48,128]{3,2,1,0:T(8,128)(2,1)S(1)}, u32[]{:S(2)}, u32[]{:S(2)}) async-start(bf16[32,3,48,128]{3,2,1,0:T(8,128)(2,1)} %bitcast.385), calls=%async_computation | async-start | bytes 2359296 | tf_op jit(solution)/shard_map/all_to_all | solution.py:122
  142.7 63.0 %all-to-all-start.2 = ((bf16[32,3,48,128]{3,2,1,0:T(8,128)(2,1)}), bf16[32,3,48,128]{3,2,1,0:T(8,128)(2,1)}, u32[]{:S(2)}, u32[]{:S(2)}) async-start(bf16[32,3,48,128]{3,2,1,0:T(8,128)(2,1)} %bitcast.386), calls=%async_computation.2 | async-start | bytes 2359296 | tf_op jit(solution)/shard_map/all_to_all | solution.py:124
  240.3 5.4 copy-start.6
  240.3 5.5 copy-start.9
  240.3 5.6 copy-start.4
  240.3 5.6 copy-start.1
  240.3 5.6 copy-start.2
  240.3 79.9 %all-to-all-start.3 = ((bf16[1,3,1536,128]{3,1,0,2:T(4,128)(2,1)}), bf16[1,3,1536,128]{3,1,0,2:T(4,128)(2,1)S(1)}, u32[]{:S(2)}, u32[]{:S(2)}) async-start(bf16[1,3,1536,128]{3,1,0,2:T(4,128)(2,1)} %bitcast.350), calls=%async_computation.3 | async-start | bytes 3145728 | tf_op jit(solution)/shard_map/all_to_all | solution.py:126
  323.9 22.1 %copy-start.7 = (bf16[3072,64]{0,1:T(8,128)(2,1)S(1)}, bf16[3072,64]{0,1:T(8,128)(2,1)}, u32[]{:S(2)}) copy-start(bf16[3072,64]{0,1:T(8,128)(2,1)} %param.23) | copy-start | bytes 1179652
  323.9 22.1 %copy-start.10 = (f32[64]{0:T(128)S(1)}, f32[64]{0:T(128)}, u32[]{:S(2)}) copy-start(f32[64]{0:T(128)} %param.24) | copy-start | bytes 772
  347.6 1.1 copy-start.3
  347.6 46.3 %copy-start.5 = (f32[512]{0:T(512)S(1)}, f32[512]{0:T(512)}, u32[]{:S(2)}) copy-start(f32[512]{0:T(512)} %param.30) | copy-start | bytes 6148
  387.2 6.8 %collective-permute-start = (bf16[4,3,1,512]{3,2,1,0:T(2,128)(2,1)S(1)}, bf16[4,3,1,512]{3,2,1,0:T(2,128)(2,1)S(1)}, u32[]{:S(2)}, u32[]{:S(2)}) collective-permute-start(bf16[4,3,1,512]{3,2,1,0:T(2,128)(2,1)S(1)} %get-tuple-element.89), channel_id=1, source_target_pairs={{0,8},{8,16},{16,24},{24,32},{32,40},{40,48},{48,56},{56,64},{64,7... | collective-permute-start | bytes 36872 | tf_op jit(solution)/shard_map/ppermute | solution.py:37
  392.3 5.7 %collective-permute-start.1 = (bf16[4,3,1,512]{3,2,1,0:T(2,128)(2,1)S(1)}, bf16[4,3,1,512]{3,2,1,0:T(2,128)(2,1)S(1)}, u32[]{:S(2)}, u32[]{:S(2)}) collective-permute-start(bf16[4,3,1,512]{3,2,1,0:T(2,128)(2,1)S(1)} %get-tuple-element.90), channel_id=1, source_target_pairs={{8,0},{16,8},{24,16},{32,24},{40,32},{48,40},{56,48},{64,56},{72,6... | collective-permute-start | bytes 36872 | tf_op jit(solution)/shard_map/ppermute | solution.py:39
  426.1 2.5 copy-start.8
